TPU v7x, 256 devices: a whole 4x4x8 slice. The times are simulated.
256 devices in a mesh: section: 4 (over x_lo, core), dp: 8 (over y, x_hi), expert: 8 (over z).
Axes of the slice: x: 4 (x_hi: 2, x_lo: 2; x = x_hi * 2 + x_lo), y: 4, z: 8, core: 2. Of those that a mesh axis runs over, the one named last changes fastest.
Arguments:
- incoming: bfloat16 [4, 2, 1024, 3584], P('section', None, ('dp', 'expert')), may hold values from -6 to 6
- stash: bfloat16 [4, 2, 1024, 3584], P('section', None, ('dp', 'expert')), may hold values from -6 to 6
- expert_ids: int32 [4, 2, 1024, 2], P('section', None, ('dp', 'expert')), may hold values from 0 to 7, all different within a row; in each aligned block of 16 rows (0 to 15, 16 to 31, ..., all dimensions but the last counted through in order) at most 6 rows name the same one
- route_weight: float32 [4, 2, 1024, 2], P('section', None, ('dp', 'expert')), may hold values from 0.1 to 1
- w_gate: bfloat16 [4, 8, 3584, 2048], P('section', 'expert', None, 'dp'), may hold values from -0.09375 to 0.09375
- w_up: bfloat16 [4, 8, 3584, 2048], P('section', 'expert', None, 'dp'), may hold values from -0.09375 to 0.09375
- w_down: bfloat16 [4, 8, 2048, 3584], P('section', 'expert', 'dp'), may hold values from -0.125 to 0.125
Outputs:
- input_grad: bfloat16 [4, 2, 1024, 3584], P('section', None, ('dp', 'expert'))
- grad_gate: bfloat16 [4, 8, 3584, 2048], P('section', 'expert', None, 'dp')
- grad_up: bfloat16 [4, 8, 3584, 2048], P('section', 'expert', None, 'dp')
- grad_down: bfloat16 [4, 8, 2048, 3584], P('section', 'expert', 'dp')
Inputs may be any that keep to these rules, and one draw needn't show every extreme that they name: `expert_ids`: each token names 2 different experts. Among the 16 tokens of one device in one micro-batch (aligned blocks of rows), no expert is named by more than 6 of them, a bound that some block reaches.
All inputs are finite; a program needn't handle non-finite values.
Results may differ from a plain program's by a relative error of at most 0.01.
Values may be sent and summed in bfloat16 or wider, within the bound.
No kernel may reach another device: no remote copies, remote signals or barrier semaphores. Data moves between devices by JAX's collectives and lax.ppermute only.
A program may use at most 128 MiB of HBM per device.

v0:
```python
import jax
import jax.numpy as jnp
from jax import lax
from jax.sharding import PartitionSpec as P


def passed_along(x, axis, by):
    length = lax.axis_size(axis)
    return lax.ppermute(x, axis, [(i, (i + by) % length) for i in range(length)])


def slice_backward(pair_inputs, pair_scaled, gate_slice, up_slice, down_slice):
    contract_rows = (((0,), (0,)), ((), ()))
    contract_last = (((1,), (1,)), ((), ()))
    gate_pre = jnp.dot(pair_inputs, gate_slice, preferred_element_type=jnp.float32)
    up_pre = jnp.dot(pair_inputs, up_slice, preferred_element_type=jnp.float32)
    logistic = jax.nn.sigmoid(gate_pre)
    activated = gate_pre * logistic
    hidden = (activated * up_pre).astype(jnp.bfloat16)
    hidden_grad = lax.dot_general(
        pair_scaled, down_slice, contract_last, preferred_element_type=jnp.float32
    )
    gate_grad = (hidden_grad * up_pre * logistic * (1.0 + gate_pre * (1.0 - logistic))).astype(
        jnp.bfloat16
    )
    up_grad = (hidden_grad * activated).astype(jnp.bfloat16)
    down_total = lax.dot_general(
        hidden, pair_scaled, contract_rows, preferred_element_type=jnp.float32
    )
    gate_total = lax.dot_general(
        pair_inputs, gate_grad, contract_rows, preferred_element_type=jnp.float32
    )
    up_total = lax.dot_general(
        pair_inputs, up_grad, contract_rows, preferred_element_type=jnp.float32
    )
    partial_back = lax.dot_general(
        gate_grad, gate_slice, contract_last, preferred_element_type=jnp.float32
    )
    partial_back = partial_back + lax.dot_general(
        up_grad, up_slice, contract_last, preferred_element_type=jnp.float32
    )
    return (partial_back, gate_total, up_total, down_total)


def per_device(incoming, stash, expert_ids, route_weight, w_gate, w_up, w_down):
    arrived = passed_along(incoming, "section", -1)
    upstream = arrived[0]
    tokens = stash[0]
    mbatch, tok_rows, model_width = tokens.shape
    top_count = expert_ids.shape[-1]
    experts = lax.axis_size("expert")
    replicas = lax.axis_size("dp")
    groups = replicas * experts
    capacity = max(2, 3 * tok_rows * top_count // (2 * experts))
    pair_count = tok_rows * top_count
    chosen = expert_ids[0].reshape(mbatch, pair_count)
    onehot = (chosen[:, :, None] == jnp.arange(experts, dtype=jnp.int32)[None, None, :]).astype(
        jnp.int32
    )
    running = jnp.cumsum(onehot, axis=1) - 1
    position = jnp.sum(onehot * running, axis=2)
    slot_index = chosen * capacity + position
    batch_index = jnp.arange(mbatch, dtype=jnp.int32)[:, None]
    pair_inputs = jnp.repeat(tokens, top_count, axis=1)
    weight_pairs = route_weight[0].reshape(mbatch, pair_count)
    pair_scaled = (
        weight_pairs[:, :, None] * jnp.repeat(upstream, top_count, axis=1).astype(jnp.float32)
    ).astype(jnp.bfloat16)
    empty_slots = jnp.zeros((mbatch, experts * capacity, model_width), jnp.bfloat16)
    input_slots = (
        empty_slots.at[batch_index, slot_index]
        .set(pair_inputs)
        .reshape(mbatch, experts, capacity, model_width)
    )
    scaled_slots = (
        empty_slots.at[batch_index, slot_index]
        .set(pair_scaled)
        .reshape(mbatch, experts, capacity, model_width)
    )
    tiled_shape = (mbatch, replicas, experts, capacity, model_width)
    tiled_inputs = jnp.broadcast_to(input_slots[:, None], tiled_shape).reshape(
        mbatch, groups, capacity, model_width
    )
    tiled_scaled = jnp.broadcast_to(scaled_slots[:, None], tiled_shape).reshape(
        mbatch, groups, capacity, model_width
    )
    recv_inputs, recv_scaled = (
        lax.all_to_all(tiled_inputs, ("dp", "expert"), split_axis=1, concat_axis=1, tiled=True),
        lax.all_to_all(tiled_scaled, ("dp", "expert"), split_axis=1, concat_axis=1, tiled=True),
    )
    row_total = mbatch * groups * capacity
    input_rows = recv_inputs.reshape(row_total, model_width)
    scaled_rows = recv_scaled.reshape(row_total, model_width)
    gate_slice = w_gate[0, 0]
    up_slice = w_up[0, 0]
    down_slice = w_down[0, 0]
    partial_rows, gate_total, up_total, down_total = slice_backward(
        input_rows, scaled_rows, gate_slice, up_slice, down_slice
    )
    sent_back = partial_rows.astype(jnp.bfloat16).reshape(mbatch, groups, capacity, model_width)
    returned = lax.all_to_all(sent_back, ("dp", "expert"), split_axis=1, concat_axis=1, tiled=True)
    summed = jnp.sum(
        returned.reshape(mbatch, replicas, experts, capacity, model_width).astype(jnp.float32),
        axis=1,
    )
    pair_back = lax.optimization_barrier(summed.astype(jnp.bfloat16))
    back_flat = pair_back.reshape(mbatch, experts * capacity, model_width)
    per_pair = (
        back_flat[batch_index, slot_index]
        .astype(jnp.float32)
        .reshape(mbatch, tok_rows, top_count, model_width)
    )
    input_grad = (upstream.astype(jnp.float32) + jnp.sum(per_pair, axis=2)).astype(jnp.bfloat16)
    grad_gate = gate_total.astype(jnp.bfloat16)[None, None]
    grad_up = up_total.astype(jnp.bfloat16)[None, None]
    grad_down = down_total.astype(jnp.bfloat16)[None, None]
    return (input_grad[None], grad_gate, grad_up, grad_down)


def solution(mesh):
    return jax.shard_map(
        per_device,
        mesh=mesh,
        in_specs=(
            P("section", None, ("dp", "expert"), None),
            P("section", None, ("dp", "expert"), None),
            P("section", None, ("dp", "expert"), None),
            P("section", None, ("dp", "expert"), None),
            P("section", "expert", None, "dp"),
            P("section", "expert", None, "dp"),
            P("section", "expert", "dp", None),
        ),
        out_specs=(
            P("section", None, ("dp", "expert"), None),
            P("section", "expert", None, "dp"),
            P("section", "expert", None, "dp"),
            P("section", "expert", "dp", None),
        ),
        check_vma=False,
    )
```

profile of v0, /device:TPU:8, one launch (start us, length us, event | category | flops | bytes accessed | tf_op | source)
XLA Modules:
  0.0 493.5 jit_solution(15290916588645689784)
XLA Ops:
  0.6 0.0 copy-start
  0.6 0.8 broadcast_multiply_fusion
  1.5 0.8 copy.29
  2.2 0.1 copy.28
  2.3 0.1 mul.52
  2.4 0.1 eq.15
  2.5 0.1 fusion.15
  2.6 0.1 reduce_window_sum.11
  2.6 0.2 select_reduce_fusion
  2.8 0.1 reshape.91
  2.9 1.2 broadcast_in_dim.54
  4.1 0.2 reshape.99
  4.3 9.2 %scatter_fusion.1 = bf16[2,48,3584]{2,1,0:T(8,128)(2,1)S(1)} fusion(bf16[2,48,3584]{2,1,0:T(8,128)(2,1)S(1)} %broadcast_in_dim.22.clone, s32[64]{0:T(128)S(1)} %reshape.91, bf16[64,3584]{1,0:T(8,128)(2,1)S(1)} %reshape.99), kind=kCustom, calls=%fused_computation.2 | custom fusion | bytes 1376768 | tf_op jit(solution)/shard_map/scatter | solution.py:72
  13.5 0.7 copy.33
  14.2 5.2 %broadcast_in_dim.56 = bf16[2,8,8,6,3584]{4,0,3,2,1:T(2,128)(2,1)} broadcast(bf16[2,8,6,3584]{3,0,2,1:T(2,128)(2,1)S(1)} %bitcast.72), dimensions={0,2,3,4} | broadcast | bytes 6193152 | tf_op jit(solution)/shard_map/broadcast_in_dim | solution.py:81
  19.5 14.9 %all-to-all-start.1 = ((bf16[2,64,6,3584]{3,0,2,1:T(2,128)(2,1)}), bf16[2,64,6,3584]{3,0,2,1:T(2,128)(2,1)}, u32[]{:S(2)}, u32[]{:S(2)}) async-start(bf16[2,64,6,3584]{3,0,2,1:T(2,128)(2,1)} %bitcast.65), calls=%async_computation.1 | async-start | bytes 11010048 | tf_op jit(solution)/shard_map/all_to_all | solution.py:88
  34.3 0.0 copy-done.10
  34.3 0.6 collective-permute-start
  35.0 0.0 copy-done.9
  35.0 0.1 copy.30
  35.1 0.1 mul.54
  35.1 15.4 %collective-permute-done = bf16[1,2,16,3584]{3,2,1,0:T(8,128)(2,1)S(1)} collective-permute-done((bf16[1,2,16,3584]{3,2,1,0:T(8,128)(2,1)S(1)}, bf16[1,2,16,3584]{3,2,1,0:T(8,128)(2,1)S(1)}, u32[]{:S(2)}, u32[]{:S(2)}) %collective-permute-start) | collective-permute-done | bytes 229408 | tf_op jit(solution)/shard_map/ppermute | solution.py:9
  50.6 1.2 broadcast_in_dim.24
  51.8 1.8 convert_element_type.58
  53.7 0.9 multiply_convert_fusion
  54.6 11.8 %scatter_fusion = bf16[2,48,3584]{2,1,0:T(8,128)(2,1)S(1)} fusion(bf16[2,48,3584]{2,1,0:T(8,128)(2,1)S(1)} %broadcast_in_dim.22.clone.1, s32[64]{0:T(128)S(1)} %reshape.91, bf16[64,3584]{1,0:T(8,128)(2,1)} %bitcast.74), kind=kCustom, calls=%fused_computation.1 | custom fusion | bytes 1376768 | tf_op jit(solution)/shard_map/scatter | solution.py:77
  66.4 0.7 copy.31
  67.1 92.3 %all-to-all-done.1 = bf16[2,64,6,3584]{3,0,2,1:T(2,128)(2,1)} async-done(((bf16[2,64,6,3584]{3,0,2,1:T(2,128)(2,1)}), bf16[2,64,6,3584]{3,0,2,1:T(2,128)(2,1)}, u32[]{:S(2)}, u32[]{:S(2)}) %all-to-all-start.1) | async-done | bytes 5505056 | tf_op jit(solution)/shard_map/all_to_all | solution.py:88
  159.5 5.3 %broadcast_in_dim.26 = bf16[2,8,8,6,3584]{4,0,3,2,1:T(2,128)(2,1)} broadcast(bf16[2,8,6,3584]{3,0,2,1:T(2,128)(2,1)S(1)} %bitcast.71), dimensions={0,2,3,4} | broadcast | bytes 6193152 | tf_op jit(solution)/shard_map/broadcast_in_dim | solution.py:84
  164.7 7.8 %all-to-all-start = ((bf16[2,64,6,3584]{3,0,2,1:T(2,128)(2,1)}), bf16[2,64,6,3584]{3,0,2,1:T(2,128)(2,1)}, u32[]{:S(2)}, u32[]{:S(2)}) async-start(bf16[2,64,6,3584]{3,0,2,1:T(2,128)(2,1)} %bitcast.66), calls=%async_computation | async-start | bytes 11010048 | tf_op jit(solution)/shard_map/all_to_all | solution.py:89
  172.5 6.6 %copy.34 = bf16[2,64,6,3584]{3,2,1,0:T(8,128)(2,1)} copy(bf16[2,64,6,3584]{3,0,2,1:T(2,128)(2,1)} %all-to-all-done.1) | data formatting | bytes 11010048 | tf_op jit(solution)/shard_map/all_to_all | solution.py:88
  179.1 9.7 %reshape.79 = bf16[768,3584]{1,0:T(8,128)(2,1)} reshape(bf16[2,64,6,3584]{3,2,1,0:T(8,128)(2,1)} %copy.34) | data formatting | bytes 11010048 | tf_op jit(solution)/shard_map/reshape | solution.py:92
  188.8 0.0 copy-done
  188.8 4.3 fusion.5
  193.1 0.4 copy-done.3
  193.5 2.5 fusion.8
  196.0 101.1 %all-to-all-done = bf16[2,64,6,3584]{3,0,2,1:T(2,128)(2,1)} async-done(((bf16[2,64,6,3584]{3,0,2,1:T(2,128)(2,1)}), bf16[2,64,6,3584]{3,0,2,1:T(2,128)(2,1)}, u32[]{:S(2)}, u32[]{:S(2)}) %all-to-all-start) | async-done | bytes 5505056 | tf_op jit(solution)/shard_map/all_to_all | solution.py:89
  297.1 6.6 %copy.32 = bf16[2,64,6,3584]{3,2,1,0:T(8,128)(2,1)} copy(bf16[2,64,6,3584]{3,0,2,1:T(2,128)(2,1)} %all-to-all-done) | data formatting | bytes 11010048 | tf_op jit(solution)/shard_map/all_to_all | solution.py:89
  303.7 9.7 %reshape.76 = bf16[768,3584]{1,0:T(8,128)(2,1)} reshape(bf16[2,64,6,3584]{3,2,1,0:T(8,128)(2,1)} %copy.32) | data formatting | bytes 11010048 | tf_op jit(solution)/shard_map/reshape | solution.py:93
  313.4 5.0 %multiply_convert_fusion.2 = (bf16[768,256]{1,0:T(8,128)(2,1)S(1)}, bf16[768,256]{1,0:T(8,128)(2,1)S(1)}) fusion(f32[768,256]{1,0:T(8,128)S(1)} %fusion.5, f32[768,256]{1,0:T(8,128)} %fusion.8, bf16[768,3584]{1,0:T(8,128)(2,1)} %reshape.76, bf16[1,1,256,3584]{3,2,1,0:T(8,128)(2,1)} %param.13), kind=kOutput, calls=%fused_computation.21 | convolution fusion | flops 1411842048 | bytes 9699328 | tf_op jit(solution)/shard_map/dot_general | solution.py:20
  318.4 0.0 copy-start.7
  318.4 0.0 copy-start.4
  318.4 1.6 fusion.3
  320.0 4.1 add_convert_fusion
  324.1 9.6 %reshape.80 = bf16[2,64,6,3584]{3,2,1,0:T(8,128)(2,1)} reshape(bf16[768,3584]{1,0:T(8,128)(2,1)} %add_convert_fusion) | data formatting | bytes 11010048 | tf_op jit(solution)/shard_map/reshape | solution.py:100
  333.6 11.9 %copy.35 = bf16[2,64,6,3584]{3,0,2,1:T(2,128)(2,1)} copy(bf16[2,64,6,3584]{3,2,1,0:T(8,128)(2,1)} %reshape.80) | data formatting | bytes 11010048 | tf_op jit(solution)/shard_map/reshape | solution.py:100
  345.5 7.6 %all-to-all-start.2 = ((bf16[2,64,6,3584]{3,0,2,1:T(2,128)(2,1)}), bf16[2,64,6,3584]{3,0,2,1:T(2,128)(2,1)}, u32[]{:S(2)}, u32[]{:S(2)}) async-start(bf16[2,64,6,3584]{3,0,2,1:T(2,128)(2,1)} %copy.35), calls=%async_computation.2 | async-start | bytes 11010048 | tf_op jit(solution)/shard_map/all_to_all | solution.py:101
  353.2 0.1 reshape.85
  353.3 5.6 %fusion.1 = bf16[1,1,3584,256]{3,2,1,0:T(8,128)(2,1)} fusion(bf16[768,3584]{1,0:T(8,128)(2,1)} %reshape.79, bf16[768,256]{1,0:T(8,128)(2,1)S(1)} %copy-done.8), kind=kOutput, calls=%fused_computation.8 | convolution fusion | flops 1410203648 | bytes 7733248 | tf_op jit(solution)/shard_map/dot_general | solution.py:33
  358.9 0.0 copy-start.13
  358.9 2.9 fusion
  361.8 0.0 copy-done.13
  361.8 3.0 fusion.2
  364.7 113.1 %all-to-all-done.2 = bf16[2,64,6,3584]{3,0,2,1:T(2,128)(2,1)} async-done(((bf16[2,64,6,3584]{3,0,2,1:T(2,128)(2,1)}), bf16[2,64,6,3584]{3,0,2,1:T(2,128)(2,1)}, u32[]{:S(2)}, u32[]{:S(2)}) %all-to-all-start.2) | async-done | bytes 5505056 | tf_op jit(solution)/shard_map/all_to_all | solution.py:101
  477.9 8.0 %reduce_sum.36 = bf16[2,8,6,3584]{3,0,2,1:T(2,128)(2,1)S(1)} reduce(bf16[2,8,8,6,3584]{4,0,3,2,1:T(2,128)(2,1)} %bitcast.11, bf16[]{:T(256)} %constant.7.clone.1), dimensions={1}, to_apply=%region_4.5 | reduce | flops 2408448 | bytes 6193154 | tf_op jit(solution)/shard_map/reduce_sum | solution.py:102
  485.9 0.0 copy-start.6
  485.9 0.0 copy-start.1
  485.9 0.1 copy.39
  486.0 0.7 copy.37
  486.7 0.1 copy.38
  486.8 3.1 gather_fusion
  489.8 1.6 reshape.84
  491.4 1.1 reduce_sum.37
  492.5 0.7 fusion.13
  (31 shorter events, 0.2 us)
Async XLA Ops:
  0.6 188.1 %copy-start = (bf16[1,1,3584,256]{3,2,1,0:T(8,128)(2,1)S(1)}, bf16[1,1,3584,256]{3,2,1,0:T(8,128)(2,1)}, u32[]{:S(2)}) copy-start(bf16[1,1,3584,256]{3,2,1,0:T(8,128)(2,1)} %param.11) | copy-start | bytes 5505028
  19.5 14.9 %copy-start.10 = (bf16[1,2,16,3584]{3,2,1,0:T(8,128)(2,1)S(1)}, bf16[1,2,16,3584]{3,2,1,0:T(8,128)(2,1)}, u32[]{:S(2)}) copy-start(bf16[1,2,16,3584]{3,2,1,0:T(8,128)(2,1)} %param.7) | copy-start | bytes 688132
  19.5 15.5 %copy-start.9 = (f32[1,2,16,2]{2,3,1,0:T(2,128)S(1)}, f32[1,2,16,2]{2,3,1,0:T(2,128)}, u32[]{:S(2)}) copy-start(f32[1,2,16,2]{2,3,1,0:T(2,128)} %param.10) | copy-start | bytes 772
  19.5 140.0 %all-to-all-start.1 = ((bf16[2,64,6,3584]{3,0,2,1:T(2,128)(2,1)}), bf16[2,64,6,3584]{3,0,2,1:T(2,128)(2,1)}, u32[]{:S(2)}, u32[]{:S(2)}) async-start(bf16[2,64,6,3584]{3,0,2,1:T(2,128)(2,1)} %bitcast.65), calls=%async_computation.1 | async-start | bytes 11010048 | tf_op jit(solution)/shard_map/all_to_all | solution.py:88
  34.3 16.2 %collective-permute-start = (bf16[1,2,16,3584]{3,2,1,0:T(8,128)(2,1)S(1)}, bf16[1,2,16,3584]{3,2,1,0:T(8,128)(2,1)S(1)}, u32[]{:S(2)}, u32[]{:S(2)}) collective-permute-start(bf16[1,2,16,3584]{3,2,1,0:T(8,128)(2,1)S(1)} %copy-done.10), channel_id=1, source_target_pairs={{0,192},{64,0},{128,64},{192,128},{1,193},{65,1},{129,65},{193,129... | collective-permute-start | bytes 688136 | tf_op jit(solution)/shard_map/ppermute | solution.py:9
  50.6 4.0 copy-start.5
  164.7 132.3 %all-to-all-start = ((bf16[2,64,6,3584]{3,0,2,1:T(2,128)(2,1)}), bf16[2,64,6,3584]{3,0,2,1:T(2,128)(2,1)}, u32[]{:S(2)}, u32[]{:S(2)}) async-start(bf16[2,64,6,3584]{3,0,2,1:T(2,128)(2,1)} %bitcast.66), calls=%async_computation | async-start | bytes 11010048 | tf_op jit(solution)/shard_map/all_to_all | solution.py:89
  188.8 4.3 copy-start.2
  188.8 4.8 copy-start.3
  193.5 119.8 %copy-start.11 = (f32[768,256]{1,0:T(8,128)}, f32[768,256]{1,0:T(8,128)S(1)}, u32[]{:S(2)}) copy-start(f32[768,256]{1,0:T(8,128)S(1)} %fusion.5) | copy-start | bytes 2359300
  318.4 1.7 copy-start.7
  318.4 1.7 copy-start.4
  345.5 7.7 %copy-start.8 = (bf16[768,256]{1,0:T(8,128)(2,1)S(1)}, bf16[768,256]{1,0:T(8,128)(2,1)}, u32[]{:S(2)}) copy-start(bf16[768,256]{1,0:T(8,128)(2,1)} %copy-done.7) | copy-start | bytes 1179652
  345.5 13.3 %slice-start = ((s8[5505024]{0:T(1024)(128)(4,1)}), s8[1310720]{0:T(1024)(128)(4,1)S(1)}, s32[]{:S(2)}) async-start(s8[5505024]{0:T(1024)(128)(4,1)} %bitcast.67), calls=%async_computation.3 | async-start | bytes 2621440
  345.5 132.3 %all-to-all-start.2 = ((bf16[2,64,6,3584]{3,0,2,1:T(2,128)(2,1)}), bf16[2,64,6,3584]{3,0,2,1:T(2,128)(2,1)}, u32[]{:S(2)}, u32[]{:S(2)}) async-start(bf16[2,64,6,3584]{3,0,2,1:T(2,128)(2,1)} %copy.35), calls=%async_computation.2 | async-start | bytes 11010048 | tf_op jit(solution)/shard_map/all_to_all | solution.py:101
  353.3 5.6 %slice-start.1 = ((s8[5505024]{0:T(1024)(128)(4,1)}), s8[4194304]{0:T(1024)(128)(4,1)S(1)}, s32[]{:S(2)}) async-start(s8[5505024]{0:T(1024)(128)(4,1)} %bitcast.67), calls=%async_computation.4 | async-start | bytes 8388608
  353.3 8.5 %slice-start.2 = ((s8[5505024]{0:T(1024)(128)(4,1)}), s8[4194304]{0:T(1024)(128)(4,1)S(1)}, s32[]{:S(2)}) async-start(s8[5505024]{0:T(1024)(128)(4,1)} %bitcast.69), calls=%async_computation.5 | async-start | bytes 8388608
  358.9 2.9 slice-start.3
  358.9 2.9 copy-start.12
  358.9 2.9 copy-start.13
  485.9 6.7 %copy-start.6 = (bf16[1,2,16,3584]{3,2,1,0:T(8,128)(2,1)S(1)}, bf16[1,2,16,3584]{3,2,1,0:T(8,128)(2,1)}, u32[]{:S(2)}) copy-start(bf16[1,2,16,3584]{3,2,1,0:T(8,128)(2,1)} %copy-done.5) | copy-start | bytes 688132
  485.9 7.4 %copy-start.1 = (bf16[1,1,3584,256]{3,2,1,0:T(8,128)(2,1)S(1)}, bf16[1,1,3584,256]{3,2,1,0:T(8,128)(2,1)}, u32[]{:S(2)}) copy-start(bf16[1,1,3584,256]{3,2,1,0:T(8,128)(2,1)} %param.11) | copy-start | bytes 5505028
where the time goes:
time: 501 us; the launch traced here: 494 us
  waiting for transfers between devices  322 us (64%)
  local copies, waits for them, and re-layouts  98.8 us (20%)
  starting transfers between devices  30.9 us (6%)
  matrix products  28.8 us (6%)
  other arithmetic  11.9 us (2%)
    all_to_all x1, waiting for transfers between devices, per_device(): lax.all_to_all(sent_back, ('dp', 'expert'), split_axis=1, concat_axis=1,...  113 us
    all_to_all x1, waiting for transfers between devices, per_device(): lax.all_to_all(tiled_scaled, ('dp', 'expert'), split_axis=1, concat_axis=...  101 us
    all_to_all x1, waiting for transfers between devices, per_device(): lax.all_to_all(tiled_inputs, ('dp', 'expert'), split_axis=1, concat_axis=...  92.3 us
    reshape x2, local copies, waits for them, and re-layouts, per_device(): partial_rows.astype(jnp.bfloat16)  21.4 us
    ppermute x1, waiting for transfers between devices, passed_along(): lax.ppermute(x, axis, [(i, (i + by) % length) for i in range(length)])  15.4 us
    all_to_all x1, starting transfers between devices, per_device(): lax.all_to_all(tiled_inputs, ('dp', 'expert'), split_axis=1, concat_axis=...  14.9 us
    scatter x2, local copies, waits for them, and re-layouts, per_device(): scaled_slots = empty_slots.at[batch_index, slot_index].set(pair_scaled).r...  12.5 us
  transfers between devices with their start and end apart: 4, of which 4 were waited for; matrix products, arithmetic and copies ran while one was open for 10% of the time, Pallas kernels for 0%

commit v1 on v0

--- a/solution.py
+++ b/solution.py
@@ -49,10 +49,9 @@
     mbatch, tok_rows, model_width = tokens.shape
     top_count = expert_ids.shape[-1]
     experts = lax.axis_size("expert")
-    replicas = lax.axis_size("dp")
-    groups = replicas * experts
     capacity = max(2, 3 * tok_rows * top_count // (2 * experts))
     pair_count = tok_rows * top_count
+    slot_count = experts * capacity
     chosen = expert_ids[0].reshape(mbatch, pair_count)
     onehot = (chosen[:, :, None] == jnp.arange(experts, dtype=jnp.int32)[None, None, :]).astype(
         jnp.int32
@@ -60,57 +59,55 @@
     running = jnp.cumsum(onehot, axis=1) - 1
     position = jnp.sum(onehot * running, axis=2)
     slot_index = chosen * capacity + position
-    batch_index = jnp.arange(mbatch, dtype=jnp.int32)[:, None]
-    pair_inputs = jnp.repeat(tokens, top_count, axis=1)
+    pair_slot = slot_index[:, :, None] == jnp.arange(slot_count, dtype=jnp.int32)[None, None, :]
+    token_slot = pair_slot.reshape(mbatch, tok_rows, top_count, slot_count).any(axis=2)
+    token_slot = token_slot.astype(jnp.bfloat16)
     weight_pairs = route_weight[0].reshape(mbatch, pair_count)
-    pair_scaled = (
-        weight_pairs[:, :, None] * jnp.repeat(upstream, top_count, axis=1).astype(jnp.float32)
-    ).astype(jnp.bfloat16)
-    empty_slots = jnp.zeros((mbatch, experts * capacity, model_width), jnp.bfloat16)
-    input_slots = (
-        empty_slots.at[batch_index, slot_index]
-        .set(pair_inputs)
-        .reshape(mbatch, experts, capacity, model_width)
+    slot_weight = jnp.sum(jnp.where(pair_slot, weight_pairs[:, :, None], 0.0), axis=1)
+
+    def to_slots(rows):
+        gathered = jnp.einsum(
+            "mts,mtd->msd", token_slot, rows, preferred_element_type=jnp.float32
+        )
+        return gathered
+
+    def by_expert(slots):
+        return (
+            slots.reshape(mbatch, experts, capacity, model_width)
+            .transpose(1, 0, 2, 3)
+            .reshape(experts, mbatch * capacity, model_width)
+        )
+
+    input_slots = by_expert(to_slots(tokens).astype(jnp.bfloat16))
+    sent_inputs = lax.all_to_all(input_slots, "expert", 0, 0, tiled=True)
+    recv_inputs = lax.all_gather(sent_inputs, "dp", axis=0, tiled=True)
+
+    scaled_slots = by_expert(
+        (slot_weight[:, :, None] * to_slots(upstream)).astype(jnp.bfloat16)
     )
-    scaled_slots = (
-        empty_slots.at[batch_index, slot_index]
-        .set(pair_scaled)
-        .reshape(mbatch, experts, capacity, model_width)
-    )
-    tiled_shape = (mbatch, replicas, experts, capacity, model_width)
-    tiled_inputs = jnp.broadcast_to(input_slots[:, None], tiled_shape).reshape(
-        mbatch, groups, capacity, model_width
-    )
-    tiled_scaled = jnp.broadcast_to(scaled_slots[:, None], tiled_shape).reshape(
-        mbatch, groups, capacity, model_width
-    )
-    recv_inputs, recv_scaled = (
-        lax.all_to_all(tiled_inputs, ("dp", "expert"), split_axis=1, concat_axis=1, tiled=True),
-        lax.all_to_all(tiled_scaled, ("dp", "expert"), split_axis=1, concat_axis=1, tiled=True),
-    )
-    row_total = mbatch * groups * capacity
-    input_rows = recv_inputs.reshape(row_total, model_width)
-    scaled_rows = recv_scaled.reshape(row_total, model_width)
+    sent_scaled = lax.all_to_all(scaled_slots, "expert", 0, 0, tiled=True)
+    recv_scaled = lax.all_gather(sent_scaled, "dp", axis=0, tiled=True)
+
+    input_rows = recv_inputs.reshape(-1, model_width)
+    scaled_rows = recv_scaled.reshape(-1, model_width)
     gate_slice = w_gate[0, 0]
     up_slice = w_up[0, 0]
     down_slice = w_down[0, 0]
     partial_rows, gate_total, up_total, down_total = slice_backward(
         input_rows, scaled_rows, gate_slice, up_slice, down_slice
     )
-    sent_back = partial_rows.astype(jnp.bfloat16).reshape(mbatch, groups, capacity, model_width)
-    returned = lax.all_to_all(sent_back, ("dp", "expert"), split_axis=1, concat_axis=1, tiled=True)
-    summed = jnp.sum(
-        returned.reshape(mbatch, replicas, experts, capacity, model_width).astype(jnp.float32),
-        axis=1,
+    sent_back = partial_rows.astype(jnp.bfloat16).reshape(recv_inputs.shape)
+    summed = lax.psum_scatter(sent_back, "dp", scatter_dimension=0, tiled=True)
+    returned = lax.all_to_all(summed, "expert", 0, 0, tiled=True)
+    back_slots = (
+        returned.reshape(experts, mbatch, capacity, model_width)
+        .transpose(1, 0, 2, 3)
+        .reshape(mbatch, slot_count, model_width)
     )
-    pair_back = lax.optimization_barrier(summed.astype(jnp.bfloat16))
-    back_flat = pair_back.reshape(mbatch, experts * capacity, model_width)
-    per_pair = (
-        back_flat[batch_index, slot_index]
-        .astype(jnp.float32)
-        .reshape(mbatch, tok_rows, top_count, model_width)
+    pair_sum = jnp.einsum(
+        "mts,msd->mtd", token_slot, back_slots, preferred_element_type=jnp.float32
     )
-    input_grad = (upstream.astype(jnp.float32) + jnp.sum(per_pair, axis=2)).astype(jnp.bfloat16)
+    input_grad = (upstream.astype(jnp.float32) + pair_sum).astype(jnp.bfloat16)
     grad_gate = gate_total.astype(jnp.bfloat16)[None, None]
     grad_up = up_total.astype(jnp.bfloat16)[None, None]
     grad_down = down_total.astype(jnp.bfloat16)[None, None]

time: 501 us -> 411 us (0.82)
  waiting for transfers between devices: 322 us -> 236 us
  blocking collectives: 0 us -> 63 us
  local copies, waits for them, and re-layouts: 98.8 us -> 54.1 us
  starting transfers between devices: 30.9 us -> 7.37 us
  between operations: 1.2 us -> 14 us
  other arithmetic: 11.9 us -> 1.2 us
    all_to_all x3 -> x1, waiting for transfers between devices: 307 us -> 13.4 us  [per_device(): returned = lax.all_to_all(summed, 'expert', 0, 0, tiled=True)]
    all_gather x0 -> x2, waiting for transfers between devices: none -> 110 us  [the longest x1 62.8 us: per_device(): recv_scaled = lax.all_gather(sent_scaled, 'dp', axis=0, tiled=True)]
    reduce_scatter x0 -> x1, waiting for transfers between devices: none -> 110 us  [per_device(): summed = lax.psum_scatter(sent_back, 'dp', scatter_dimension=0, tiled=True)]
    all_to_all x0 -> x2, blocking collectives: none -> 63 us  [the longest x1 34.2 us: per_device(): sent_inputs = lax.all_to_all(input_slots, 'expert', 0, 0, tiled=True)]
    all_to_all x3 -> x1, starting transfers between devices: 30.2 us -> 7.17 us  [per_device(): returned = lax.all_to_all(summed, 'expert', 0, 0, tiled=True)]
    scatter x4 -> x0, local copies, waits for them, and re-layouts: 22.4 us -> none  [the longest x2 12.5 us: per_device(): scaled_slots = empty_slots.at[batch_index, slot_index].set(pair_scaled).r...]
    all_gather x0 -> x2, local copies, waits for them, and re-layouts: none -> 17.2 us  [the longest x1 8.62 us: per_device(): recv_inputs = lax.all_gather(sent_inputs, 'dp', axis=0, tiled=True)]
    broadcast_in_dim x6 -> x1, local copies, waits for them, and re-layouts: 13 us -> 0.09 us  [per_device(): jnp.where(pair_slot, weight_pairs[:, :, None], 0.0)]
  transfers between devices with their start and end apart: 4 -> 5, of which waited for: 4 -> 5; matrix products, arithmetic and copies ran while one was open for 10% -> 10% of each run, Pallas kernels for 0% -> 0%
where the time goes in v1:
time: 411 us; the launch traced here: 407 us
  waiting for transfers between devices  236 us (57%)
  blocking collectives  63 us (15%)
  local copies, waits for them, and re-layouts  54.1 us (13%)
  matrix products  31.5 us (8%)
  between operations  14 us (3%)
  starting transfers between devices  7.37 us (2%)
    reduce_scatter x1, waiting for transfers between devices, per_device(): summed = lax.psum_scatter(sent_back, 'dp', scatter_dimension=0, tiled=True)  110 us
    all_gather x1, waiting for transfers between devices, per_device(): recv_scaled = lax.all_gather(sent_scaled, 'dp', axis=0, tiled=True)  62.8 us
    all_gather x1, waiting for transfers between devices, per_device(): recv_inputs = lax.all_gather(sent_inputs, 'dp', axis=0, tiled=True)  47 us
    all_to_all x1, blocking collectives, per_device(): sent_inputs = lax.all_to_all(input_slots, 'expert', 0, 0, tiled=True)  34.2 us
    all_to_all x1, blocking collectives, per_device(): sent_scaled = lax.all_to_all(scaled_slots, 'expert', 0, 0, tiled=True)  28.8 us
    all_to_all x1, waiting for transfers between devices, per_device(): returned = lax.all_to_all(summed, 'expert', 0, 0, tiled=True)  13.4 us
    reshape x1, local copies, waits for them, and re-layouts, per_device(): input_rows = recv_inputs.reshape(-1, model_width)  9.51 us
    reshape x1, local copies, waits for them, and re-layouts, per_device(): scaled_rows = recv_scaled.reshape(-1, model_width)  9.34 us
  transfers between devices with their start and end apart: 5, of which 5 were waited for; matrix products, arithmetic and copies ran while one was open for 10% of the time, Pallas kernels for 0%

profile of v1, /device:TPU:8, one launch (start us, length us, event | category | flops | bytes accessed | tf_op | source)
XLA Modules:
  0.0 407.5 jit_solution(17382456177079624147)
XLA Ops:
  7.2 0.0 copy-start
  7.2 0.0 copy-start.8
  7.2 0.0 copy-start.7
  7.2 0.0 all-gather.5.cloned.1.call-start
  7.2 0.9 copy.59
  8.1 0.1 eq.35
  8.2 0.1 fusion.20
  8.3 0.1 reduce_window_sum.11
  8.4 0.2 select_reduce_fusion.1
  8.6 0.1 reduce_sum.21
  8.6 0.1 copy.60
  8.7 0.7 bitcast_add_fusion
  9.4 0.1 fusion.21
  9.5 1.3 convolution_convert_fusion.3
  10.8 0.7 copy.67
  11.6 0.1 copy.68
  11.7 0.2 copy.69
  11.9 34.2 %all_to_all.15 = bf16[8,12,3584]{2,1,0:T(8,128)(2,1)S(1)} all-to-all(bf16[8,12,3584]{2,1,0:T(8,128)(2,1)S(1)} %copy.69), channel_id=1, replica_groups=mesh['section'=4,'dp'=8,'expert'=8] {'expert'}, dimensions={0} | all-to-all | bytes 1376256 | tf_op jit(solution)/shard_map/all_to_all | solution.py:82
  46.1 1.2 copy.70
  47.3 0.0 all-gather.5.cloned.1.call-update
  47.3 0.0 all-gather.3.cloned.1.call-start
  47.4 0.1 collective-permute-start
  47.5 0.1 copy.61
  47.6 0.1 broadcast_in_dim.30
  47.7 0.1 select_reduce_fusion
  47.8 3.2 collective-permute-done
  51.0 0.4 fusion.3
  51.4 0.7 copy.62
  52.1 0.1 copy.63
  52.2 0.2 copy.64
  52.5 28.8 %all_to_all.16 = bf16[8,12,3584]{2,1,0:T(8,128)(2,1)S(1)} all-to-all(bf16[8,12,3584]{2,1,0:T(8,128)(2,1)S(1)} %copy.64), channel_id=1, replica_groups=mesh['section'=4,'dp'=8,'expert'=8] {'expert'}, dimensions={0} | all-to-all | bytes 1376256 | tf_op jit(solution)/shard_map/all_to_all | solution.py:88
  81.2 1.2 copy.65
  82.5 0.0 all-gather.3.cloned.1.call-update
  82.5 0.0 reduce-scatter.2.cloned.1.call-start
  82.5 47.0 %all-gather.5.cloned.1.call-done = bf16[64,12,3584]{2,0,1:T(8,128)(2,1)} async-done(((bf16[8,12,3584]{2,0,1:T(8,128)(2,1)}), bf16[64,12,3584]{2,0,1:T(8,128)(2,1)}) %all-gather.5.cloned.1.call-update) | async-done | bytes 5505040 | tf_op jit(solution)/shard_map/all_gather | solution.py:83
  129.5 8.6 %copy.71 = bf16[64,12,3584]{2,1,0:T(8,128)(2,1)} copy(bf16[64,12,3584]{2,0,1:T(8,128)(2,1)} %all-gather.5.cloned.1.call-done) | data formatting | bytes 11010048 | tf_op jit(solution)/shard_map/all_gather | solution.py:83
  138.2 9.5 %reshape.58 = bf16[768,3584]{1,0:T(8,128)(2,1)} reshape(bf16[64,12,3584]{2,1,0:T(8,128)(2,1)} %copy.71) | data formatting | bytes 11010048 | tf_op jit(solution)/shard_map/reshape | solution.py:91
  147.7 4.3 %fusion.6 = f32[768,256]{1,0:T(8,128)S(1)} fusion(bf16[768,3584]{1,0:T(8,128)(2,1)} %reshape.58, bf16[1,1,3584,256]{3,2,1,0:T(8,128)(2,1)S(1)} %copy-done), kind=kOutput, calls=%fused_computation.12 | convolution fusion | flops 1409286144 | bytes 8126464 | tf_op jit(solution)/shard_map/dot_general | solution.py:15
  152.0 0.4 copy-done.2
  152.4 2.5 fusion.9
  154.9 62.8 %all-gather.3.cloned.1.call-done = bf16[64,12,3584]{2,0,1:T(8,128)(2,1)} async-done(((bf16[8,12,3584]{2,0,1:T(8,128)(2,1)}), bf16[64,12,3584]{2,0,1:T(8,128)(2,1)}) %all-gather.3.cloned.1.call-update) | async-done | bytes 5505040 | tf_op jit(solution)/shard_map/all_gather | solution.py:89
  217.8 8.6 %copy.66 = bf16[64,12,3584]{2,1,0:T(8,128)(2,1)} copy(bf16[64,12,3584]{2,0,1:T(8,128)(2,1)} %all-gather.3.cloned.1.call-done) | data formatting | bytes 11010048 | tf_op jit(solution)/shard_map/all_gather | solution.py:89
  226.4 9.3 %reshape.55 = bf16[768,3584]{1,0:T(8,128)(2,1)} reshape(bf16[64,12,3584]{2,1,0:T(8,128)(2,1)} %copy.66) | data formatting | bytes 11010048 | tf_op jit(solution)/shard_map/reshape | solution.py:92
  235.7 5.0 %multiply_convert_fusion.1 = (bf16[768,256]{1,0:T(8,128)(2,1)S(1)}, bf16[768,256]{1,0:T(8,128)(2,1)S(1)}) fusion(f32[768,256]{1,0:T(8,128)S(1)} %fusion.6, f32[768,256]{1,0:T(8,128)} %fusion.9, bf16[768,3584]{1,0:T(8,128)(2,1)} %reshape.55, bf16[1,1,256,3584]{3,2,1,0:T(8,128)(2,1)} %param.13), kind=kOutput, calls=%fused_computation.20 | convolution fusion | flops 1411842048 | bytes 9699328 | tf_op jit(solution)/shard_map/dot_general | solution.py:20
  240.7 0.0 copy-start.4
  240.7 0.0 copy-start.3
  240.7 1.6 fusion.4
  242.4 0.1 copy-done.3
  242.5 4.0 add_convert_fusion
  246.6 9.2 %reshape.59 = bf16[64,12,3584]{2,1,0:T(8,128)(2,1)} reshape(bf16[768,3584]{1,0:T(8,128)(2,1)} %add_convert_fusion) | data formatting | bytes 11010048 | tf_op jit(solution)/shard_map/reshape | solution.py:99
  255.8 0.0 reduce-scatter.2.cloned.1.call-update
  255.8 109.8 %reduce-scatter.2.cloned.1.call-done = bf16[8,12,3584]{2,1,0:T(8,128)(2,1)} async-done(((bf16[64,12,3584]{2,1,0:T(8,128)(2,1)}), bf16[8,12,3584]{2,1,0:T(8,128)(2,1)}) %reduce-scatter.2.cloned.1.call-update) | async-done | bytes 688144 | tf_op jit(solution)/shard_map/reduce_scatter | solution.py:100
  365.6 7.2 %all-to-all-start.2 = ((bf16[8,12,3584]{2,1,0:T(8,128)(2,1)}), bf16[8,12,3584]{2,1,0:T(8,128)(2,1)}, u32[]{:S(2)}, u32[]{:S(2)}) async-start(bf16[8,12,3584]{2,1,0:T(8,128)(2,1)} %reduce-scatter.2.cloned.1.call-done), calls=%async_computation.3 | async-start | bytes 1835008 | tf_op jit(solution)/shard_map/all_to_all | solution.py:101
  372.8 0.0 copy-start.5
  372.8 0.0 slice-start.2
  372.8 5.6 %fusion.1 = bf16[1,1,3584,256]{3,2,1,0:T(8,128)(2,1)} fusion(bf16[768,3584]{1,0:T(8,128)(2,1)} %reshape.58, bf16[768,256]{1,0:T(8,128)(2,1)} %copy-done.6), kind=kOutput, calls=%fused_computation.5 | convolution fusion | flops 1410203648 | bytes 7733248 | tf_op jit(solution)/shard_map/dot_general | solution.py:33
  378.5 0.0 slice-start.3
  378.5 0.0 copy-start.11
  378.5 2.9 fusion
  381.4 2.9 fusion.2
  384.4 13.4 %all-to-all-done.2 = bf16[8,12,3584]{2,1,0:T(8,128)(2,1)} async-done(((bf16[8,12,3584]{2,1,0:T(8,128)(2,1)}), bf16[8,12,3584]{2,1,0:T(8,128)(2,1)}, u32[]{:S(2)}, u32[]{:S(2)}) %all-to-all-start.2) | async-done | bytes 688160 | tf_op jit(solution)/shard_map/all_to_all | solution.py:101
  397.7 1.6 copy.72
  399.3 0.7 copy.73
  400.0 0.9 fusion.16
  (24 shorter events, 0.0 us)
Async XLA Ops:
  7.2 140.5 %copy-start = (bf16[1,1,3584,256]{3,2,1,0:T(8,128)(2,1)S(1)}, bf16[1,1,3584,256]{3,2,1,0:T(8,128)(2,1)}, u32[]{:S(2)}) copy-start(bf16[1,1,3584,256]{3,2,1,0:T(8,128)(2,1)} %param.11) | copy-start | bytes 5505028
  7.2 40.2 %copy-start.8 = (bf16[1,2,16,3584]{3,2,1,0:T(8,128)(2,1)S(1)}, bf16[1,2,16,3584]{3,2,1,0:T(8,128)(2,1)}, u32[]{:S(2)}) copy-start(bf16[1,2,16,3584]{3,2,1,0:T(8,128)(2,1)} %param.7) | copy-start | bytes 688132
  7.2 40.3 %copy-start.7 = (f32[1,2,16,2]{2,3,1,0:T(2,128)S(1)}, f32[1,2,16,2]{2,3,1,0:T(2,128)}, u32[]{:S(2)}) copy-start(f32[1,2,16,2]{2,3,1,0:T(2,128)} %param.10) | copy-start | bytes 772
  7.2 122.3 %all-gather.5.cloned.1.call-start = ((), (), s32[]{:S(2)}) async-start(), calls=%async_computation.5 | async-start | bytes 6193152 | tf_op jit(solution)/shard_map/all_gather | solution.py:83
  47.3 170.4 %all-gather.3.cloned.1.call-start = ((), (), s32[]{:S(2)}) async-start(), calls=%async_computation.4 | async-start | bytes 6193152 | tf_op jit(solution)/shard_map/all_gather | solution.py:89
  47.4 3.6 collective-permute-start
  82.5 283.2 %reduce-scatter.2.cloned.1.call-start = ((), (), s32[]{:S(2)}) async-start(), calls=%async_computation.6 | async-start | bytes 8257536 | tf_op jit(solution)/shard_map/reduce_scatter | solution.py:100
  147.7 4.3 %copy-start.1 = (bf16[768,3584]{1,0:T(8,128)(2,1)S(1)}, bf16[768,3584]{1,0:T(8,128)(2,1)}, u32[]{:S(2)}) copy-start(bf16[768,3584]{1,0:T(8,128)(2,1)} %reshape.58) | copy-start | bytes 16515076
  147.7 4.8 %copy-start.2 = (bf16[1,1,3584,256]{3,2,1,0:T(8,128)(2,1)S(1)}, bf16[1,1,3584,256]{3,2,1,0:T(8,128)(2,1)}, u32[]{:S(2)}) copy-start(bf16[1,1,3584,256]{3,2,1,0:T(8,128)(2,1)} %param.12) | copy-start | bytes 5505028
  152.4 83.3 %copy-start.9 = (f32[768,256]{1,0:T(8,128)}, f32[768,256]{1,0:T(8,128)S(1)}, u32[]{:S(2)}) copy-start(f32[768,256]{1,0:T(8,128)S(1)} %fusion.6) | copy-start | bytes 2359300
  240.7 1.7 copy-start.4
  240.7 1.7 copy-start.6
  240.7 1.8 copy-start.3
  365.6 12.8 %slice-start = ((s8[5505024]{0:T(1024)(128)(4,1)}), s8[1310720]{0:T(1024)(128)(4,1)S(1)}, s32[]{:S(2)}) async-start(s8[5505024]{0:T(1024)(128)(4,1)} %bitcast.61), calls=%async_computation.7 | async-start | bytes 2621440
  365.6 32.1 %all-to-all-start.2 = ((bf16[8,12,3584]{2,1,0:T(8,128)(2,1)}), bf16[8,12,3584]{2,1,0:T(8,128)(2,1)}, u32[]{:S(2)}, u32[]{:S(2)}) async-start(bf16[8,12,3584]{2,1,0:T(8,128)(2,1)} %reduce-scatter.2.cloned.1.call-done), calls=%async_computation.3 | async-start | bytes 1835008 | tf_op jit(solution)/shard_map/all_to_all | solution.py:101
  372.8 5.7 %slice-start.1 = ((s8[5505024]{0:T(1024)(128)(4,1)}), s8[4194304]{0:T(1024)(128)(4,1)S(1)}, s32[]{:S(2)}) async-start(s8[5505024]{0:T(1024)(128)(4,1)} %bitcast.61), calls=%async_computation.8 | async-start | bytes 8388608
  372.8 5.7 %copy-start.5 = (bf16[768,256]{1,0:T(8,128)(2,1)S(1)}, bf16[768,256]{1,0:T(8,128)(2,1)}, u32[]{:S(2)}) copy-start(bf16[768,256]{1,0:T(8,128)(2,1)} %copy-done.4) | copy-start | bytes 1179652
  372.8 8.6 %slice-start.2 = ((s8[5505024]{0:T(1024)(128)(4,1)}), s8[4194304]{0:T(1024)(128)(4,1)S(1)}, s32[]{:S(2)}) async-start(s8[5505024]{0:T(1024)(128)(4,1)} %bitcast.63), calls=%async_computation.9 | async-start | bytes 8388608
  378.5 2.9 slice-start.3
  378.5 2.9 copy-start.10
  378.5 2.9 copy-start.11
Sparse Core Ops, SparseCore 0:
  47.5 82.0 all-gather.4
  132.7 84.9 all-gather.2
  255.9 109.6 reduce-scatter.1
